TPU v7x, 32 devices: a whole 2x2x4 slice. The times are simulated.
32 devices in a mesh: atoms: 8 (over y, x, core), bands: 4 (over z).
Axes of the slice: x: 2, y: 2, z: 4, core: 2. Of those that a mesh axis runs over, the one named last changes fastest.
Arguments:
- subspace: bfloat16 [512, 6144], P('bands', 'atoms'), may hold values from -120 to 120
- diag_block: bfloat16 [6144, 768], P('atoms'), may hold values from -0.0625 to 0.0625
- pair_block: bfloat16 [2, 6144, 768], P(None, 'atoms'), may hold values from -0.0625 to 0.0625
- pair_pattern: int32 [2, 32, 4], P(None, 'atoms'), may hold values 0 or 1
- atom_sizes: int32 [8, 4], replicated, may hold values from 1 to 256, 768 in all within a row
- rotations: bfloat16 [4, 512, 512], P(None, None, 'bands'), may hold values from -0.25 to 0.25
Outputs:
- rotated: float32 [512, 6144], P('bands', 'atoms')
Inputs may be any that keep to these rules, and one draw needn't show every extreme that they name: `atom_sizes`: each row holds the orbital counts of the 4 atoms of one partition in order and sums to 768.
All inputs are finite; a program needn't handle non-finite values. No bound on the sum of `pair_pattern` on one device may be relied on, other than what follows from the above.
Results may differ from a plain program's by a relative error of at most 0.028.
Values may be sent and summed in bfloat16 or wider, within the bound.
No kernel may reach another device: no remote copies, remote signals or barrier semaphores. Data moves between devices by JAX's collectives and lax.ppermute only.
A program may use at most 64 MiB of HBM per device.

v0:
```python
import jax
import jax.numpy as jnp
from jax import lax
from jax.sharding import PartitionSpec as P

ROUNDS = 2
DEGREE = 8
ROTS = 4
filter_center = 0.1
filter_half = 1.25
norm_eps = 1e-06


def swapped(value, axis, stride):
    mask = 2**stride
    pairs = [(source, source ^ mask) for source in range(lax.axis_size(axis))]
    return lax.ppermute(value, axis, pairs)


def atom_onehot(atom_counts, length_total):
    atom_ends = jnp.cumsum(atom_counts, axis=-1)
    atom_starts = atom_ends - atom_counts
    positions = jnp.arange(length_total, dtype=jnp.int32)
    inside = (positions >= atom_starts[..., None]) & (positions < atom_ends[..., None])
    return inside.astype(jnp.float32)


def diagonal_weights(onehot_rows):
    levels = jnp.arange(onehot_rows.shape[0], dtype=jnp.float32)
    atom_index = jnp.sum(onehot_rows * levels[:, None], axis=0)
    upper_flag = (atom_index[:, None] < atom_index[None, :]).astype(jnp.float32)
    same_atom = (atom_index[:, None] == atom_index[None, :]).astype(jnp.float32)
    return upper_flag + 0.5 * same_atom


def apply_operator(values, diag_sym, coupling):
    result = jnp.dot(values, diag_sym, preferred_element_type=jnp.float32)
    for round_index in range(ROUNDS):
        pair_mat = coupling[round_index]
        other_rows = swapped(values, "atoms", round_index)
        own_term = lax.dot_general(
            other_rows, pair_mat, (((1,), (1,)), ((), ())), preferred_element_type=jnp.float32
        )
        sent_term = jnp.dot(values, pair_mat, preferred_element_type=jnp.float32)
        returned = swapped(sent_term.astype(jnp.bfloat16), "atoms", round_index).astype(
            sent_term.dtype
        )
        result = result + own_term + returned
    return result


def body(subspace, diag_block, pair_block, pair_pattern, atom_sizes, rotations):
    orb_dev = diag_block.shape[1]
    atoms_here = lax.axis_index("atoms")
    onehot_own = atom_onehot(
        lax.dynamic_index_in_dim(atom_sizes, atoms_here, 0, keepdims=False), orb_dev
    )
    upper_part = diag_block.astype(jnp.float32) * diagonal_weights(onehot_own)
    diag_sym = (upper_part + upper_part.T).astype(jnp.bfloat16)
    coupling = []
    for round_index in range(ROUNDS):
        partner = jnp.bitwise_xor(atoms_here, 1 << round_index)
        onehot_other = atom_onehot(
            lax.dynamic_index_in_dim(atom_sizes, partner, 0, keepdims=False), orb_dev
        )
        pattern = pair_pattern[round_index].astype(jnp.float32)
        right_side = jnp.dot(pattern, onehot_other, precision=lax.Precision.HIGHEST)
        pair_mask = lax.dot_general(
            onehot_own, right_side, (((0,), (0,)), ((), ())), precision=lax.Precision.HIGHEST
        )
        pair_mat = (pair_block[round_index].astype(jnp.float32) * pair_mask).astype(jnp.bfloat16)
        coupling.append(pair_mat)
    previous = subspace.astype(jnp.float32)
    current = (
        apply_operator(subspace, diag_sym, coupling) - filter_center * previous
    ) / filter_half
    for degree_index in range(1, DEGREE):
        applied = apply_operator(current.astype(jnp.bfloat16), diag_sym, coupling)
        following = 2.0 * (applied - filter_center * current) / filter_half - previous
        previous, current = (current, following)
    total_orbitals = orb_dev * lax.axis_size("atoms")
    basis_rows = current
    for rotation_index in range(ROTS):
        rounded = basis_rows.astype(jnp.bfloat16)
        local_cols = rotations[rotation_index]
        mixed_rows = lax.dot_general(
            local_cols,
            lax.all_gather(rounded, "bands", axis=0, tiled=True),
            (((0,), (0,)), ((), ())),
            preferred_element_type=jnp.float32,
        )
        squares = lax.psum(jnp.sum(mixed_rows * mixed_rows, axis=1), "atoms")
        col_norm = jnp.sqrt(squares / total_orbitals + norm_eps)
        basis_rows = mixed_rows / col_norm[:, None]
    return basis_rows


def solution(mesh):
    placed = (
        P("bands", "atoms"),
        P("atoms", None),
        P(None, "atoms", None),
        P(None, "atoms", None),
        P(),
        P(None, None, "bands"),
    )
    return jax.shard_map(
        body, mesh=mesh, in_specs=placed, out_specs=P("bands", "atoms"), check_vma=False
    )
```

profile of v0, /device:TPU:0, one launch (start us, length us, event | category | flops | bytes accessed | tf_op | source)
XLA Modules:
  0.0 228.8 jit_solution(13515440379078869902)
XLA Ops:
  0.0 2.9 %collective-permute-start.2 = (bf16[128,768]{1,0:T(8,128)(2,1)}, bf16[128,768]{1,0:T(8,128)(2,1)}, u32[]{:S(2)}, u32[]{:S(2)}) collective-permute-start(bf16[128,768]{1,0:T(8,128)(2,1)} %param.6), channel_id=1, source_target_pairs={{0,8},{4,12},{8,0},{12,4},{16,24},{20,28},{24,16},{28,20},{1,9},{5... | collective-permute-start | bytes 589832 | tf_op jit(solution)/shard_map/ppermute | solution.py:17
  2.9 1.0 dynamic-slice_reduce_fusion.1
  4.5 1.1 fusion.77
  5.7 2.7 %fusion.1 = bf16[768,768]{1,0:T(8,128)(2,1)S(1)} fusion(f32[768,4]{1,0:T(8,128)S(1)} %fusion.77, bf16[2,768,768]{2,1,0:T(8,128)(2,1)} %param.8, s32[4]{0:T(128)S(1)} %bitcast.155, s32[4]{0:T(128)S(1)} %bitcast_subtract_fusion.2), kind=kOutput, calls=%fused_computation.3 | convolution fusion | flops 30093312 | bytes 2371616 | tf_op jit(solution)/shard_map/dot_general | solution.py:68
  8.4 1.2 fusion.51
  10.6 1.2 fusion
  11.8 1.2 fusion.52
  13.1 1.7 copy.41
  14.9 2.0 add_multiply_fusion
  16.9 3.1 %copy.40 = f32[768,768]{0,1:T(8,128)} copy(f32[768,768]{1,0:T(8,128)} %add_multiply_fusion) | data formatting | bytes 4718592 | tf_op jit(solution)/shard_map/mul | solution.py:58
  19.9 2.7 %fusion.2 = bf16[768,768]{1,0:T(8,128)(2,1)S(1)} fusion(f32[768,768]{0,1:T(8,128)} %copy.40, f32[768]{0:T(1024)S(1)} %select_reduce_fusion, bf16[768,768]{1,0:T(8,128)(2,1)} %param.7), kind=kLoop, calls=%fused_computation.5 | loop fusion | flops 5308416 | bytes 4721664 | tf_op jit(solution)/shard_map/convert_element_type | solution.py:59
  23.2 1.4 convolution_bitcast_fusion
  24.7 1.6 multiply_convert_fusion
  26.3 0.6 convolution_convert_fusion.13
  26.9 2.1 collective-permute-start.6
  30.7 3.9 %collective-permute-done.6 = bf16[128,768]{0,1:T(8,128)(2,1)S(1)} collective-permute-done((bf16[128,768]{0,1:T(8,128)(2,1)S(1)}, bf16[128,768]{0,1:T(8,128)(2,1)S(1)}, u32[]{:S(2)}, u32[]{:S(2)}) %collective-permute-start.6) | collective-permute-done | bytes 196640 | tf_op jit(solution)/shard_map/ppermute | solution.py:17
  35.1 2.9 %collective-permute-done.7 = bf16[128,768]{0,1:T(8,128)(2,1)S(1)} collective-permute-done((bf16[128,768]{0,1:T(8,128)(2,1)S(1)}, bf16[128,768]{0,1:T(8,128)(2,1)S(1)}, u32[]{:S(2)}, u32[]{:S(2)}) %collective-permute-start.7) | collective-permute-done | bytes 196640 | tf_op jit(solution)/shard_map/ppermute | solution.py:17
  39.0 1.8 collective-permute-start.10
  42.9 2.7 %collective-permute-done.10 = bf16[128,768]{0,1:T(8,128)(2,1)S(1)} collective-permute-done((bf16[128,768]{0,1:T(8,128)(2,1)S(1)}, bf16[128,768]{0,1:T(8,128)(2,1)S(1)}, u32[]{:S(2)}, u32[]{:S(2)}) %collective-permute-start.10) | collective-permute-done | bytes 196640 | tf_op jit(solution)/shard_map/ppermute | solution.py:17
  46.1 3.2 %collective-permute-done.11 = bf16[128,768]{0,1:T(8,128)(2,1)S(1)} collective-permute-done((bf16[128,768]{0,1:T(8,128)(2,1)S(1)}, bf16[128,768]{0,1:T(8,128)(2,1)S(1)}, u32[]{:S(2)}, u32[]{:S(2)}) %collective-permute-start.11) | collective-permute-done | bytes 196640 | tf_op jit(solution)/shard_map/ppermute | solution.py:17
  50.5 1.4 collective-permute-start.14
  53.1 0.7 collective-permute-start.15
  54.3 4.0 %collective-permute-done.14 = bf16[128,768]{0,1:T(8,128)(2,1)S(1)} collective-permute-done((bf16[128,768]{0,1:T(8,128)(2,1)S(1)}, bf16[128,768]{0,1:T(8,128)(2,1)S(1)}, u32[]{:S(2)}, u32[]{:S(2)}) %collective-permute-start.14) | collective-permute-done | bytes 196640 | tf_op jit(solution)/shard_map/ppermute | solution.py:17
  58.8 2.4 %collective-permute-done.15 = bf16[128,768]{0,1:T(8,128)(2,1)S(1)} collective-permute-done((bf16[128,768]{0,1:T(8,128)(2,1)S(1)}, bf16[128,768]{0,1:T(8,128)(2,1)S(1)}, u32[]{:S(2)}, u32[]{:S(2)}) %collective-permute-start.15) | collective-permute-done | bytes 196640 | tf_op jit(solution)/shard_map/ppermute | solution.py:17
  64.1 1.5 collective-permute-start.19
  65.6 0.8 fusion.101
  66.4 3.0 %collective-permute-done.18 = bf16[128,768]{0,1:T(8,128)(2,1)S(1)} collective-permute-done((bf16[128,768]{0,1:T(8,128)(2,1)S(1)}, bf16[128,768]{0,1:T(8,128)(2,1)S(1)}, u32[]{:S(2)}, u32[]{:S(2)}) %collective-permute-start.18) | collective-permute-done | bytes 196640 | tf_op jit(solution)/shard_map/ppermute | solution.py:17
  69.9 2.4 %collective-permute-done.19 = bf16[128,768]{0,1:T(8,128)(2,1)S(1)} collective-permute-done((bf16[128,768]{0,1:T(8,128)(2,1)S(1)}, bf16[128,768]{0,1:T(8,128)(2,1)S(1)}, u32[]{:S(2)}, u32[]{:S(2)}) %collective-permute-start.19) | collective-permute-done | bytes 196640 | tf_op jit(solution)/shard_map/ppermute | solution.py:17
  73.4 0.7 collective-permute-start.22
  75.2 1.4 collective-permute-start.23
  77.2 3.1 %collective-permute-done.22 = bf16[128,768]{0,1:T(8,128)(2,1)S(1)} collective-permute-done((bf16[128,768]{0,1:T(8,128)(2,1)S(1)}, bf16[128,768]{0,1:T(8,128)(2,1)S(1)}, u32[]{:S(2)}, u32[]{:S(2)}) %collective-permute-start.22) | collective-permute-done | bytes 196640 | tf_op jit(solution)/shard_map/ppermute | solution.py:17
  80.8 2.5 %collective-permute-done.23 = bf16[128,768]{0,1:T(8,128)(2,1)S(1)} collective-permute-done((bf16[128,768]{0,1:T(8,128)(2,1)S(1)}, bf16[128,768]{0,1:T(8,128)(2,1)S(1)}, u32[]{:S(2)}, u32[]{:S(2)}) %collective-permute-start.23) | collective-permute-done | bytes 196640 | tf_op jit(solution)/shard_map/ppermute | solution.py:17
  84.4 1.4 collective-permute-start.26
  87.0 0.7 collective-permute-start.27
  88.3 2.3 collective-permute-done.26
  91.0 3.3 %collective-permute-done.27 = bf16[128,768]{0,1:T(8,128)(2,1)S(1)} collective-permute-done((bf16[128,768]{0,1:T(8,128)(2,1)S(1)}, bf16[128,768]{0,1:T(8,128)(2,1)S(1)}, u32[]{:S(2)}, u32[]{:S(2)}) %collective-permute-start.27) | collective-permute-done | bytes 196640 | tf_op jit(solution)/shard_map/ppermute | solution.py:17
  96.0 1.6 collective-permute-start.30
  99.2 4.7 %collective-permute-done.30 = bf16[128,768]{0,1:T(8,128)(2,1)S(1)} collective-permute-done((bf16[128,768]{0,1:T(8,128)(2,1)S(1)}, bf16[128,768]{0,1:T(8,128)(2,1)S(1)}, u32[]{:S(2)}, u32[]{:S(2)}) %collective-permute-start.30) | collective-permute-done | bytes 196640 | tf_op jit(solution)/shard_map/ppermute | solution.py:17
  104.4 2.4 %collective-permute-done.31 = bf16[128,768]{0,1:T(8,128)(2,1)S(1)} collective-permute-done((bf16[128,768]{0,1:T(8,128)(2,1)S(1)}, bf16[128,768]{0,1:T(8,128)(2,1)S(1)}, u32[]{:S(2)}, u32[]{:S(2)}) %collective-permute-start.31) | collective-permute-done | bytes 196640 | tf_op jit(solution)/shard_map/ppermute | solution.py:17
  107.3 18.9 %all_gather.12 = bf16[512,768]{0,1:T(8,128)(2,1)S(1)} all-gather(bf16[128,768]{0,1:T(8,128)(2,1)S(1)} %fusion.50), channel_id=1, replica_groups=mesh['atoms'=8,'bands'=4] {'bands'}, dimensions={0}, use_global_device_ids=true | all-gather | bytes 983040 | tf_op jit(solution)/shard_map/all_gather | solution.py:88
  126.6 11.8 %psum.28 = f32[128]{0:T(128)S(1)} all-reduce(f32[128]{0:T(128)S(1)} %get-tuple-element.22), channel_id=1, replica_groups=mesh['atoms'=8,'bands'=4] {'atoms'}, use_global_device_ids=true, to_apply=%region_5.6 | all-reduce | flops 128 | bytes 1024 | tf_op jit(solution)/shard_map/psum | solution.py:92
  138.5 17.6 %all_gather.13 = bf16[512,768]{0,1:T(8,128)(2,1)S(1)} all-gather(bf16[128,768]{0,1:T(8,128)(2,1)S(1)} %fusion.53), channel_id=1, replica_groups=mesh['atoms'=8,'bands'=4] {'bands'}, dimensions={0}, use_global_device_ids=true | all-gather | bytes 983040 | tf_op jit(solution)/shard_map/all_gather | solution.py:88
  156.4 11.8 %psum.29 = f32[128]{0:T(128)S(1)} all-reduce(f32[128]{0:T(128)S(1)} %get-tuple-element.24), channel_id=1, replica_groups=mesh['atoms'=8,'bands'=4] {'atoms'}, use_global_device_ids=true, to_apply=%region_7.8 | all-reduce | flops 128 | bytes 1024 | tf_op jit(solution)/shard_map/psum | solution.py:92
  168.3 17.6 %all_gather.14 = bf16[512,768]{0,1:T(8,128)(2,1)S(1)} all-gather(bf16[128,768]{0,1:T(8,128)(2,1)S(1)} %fusion.54), channel_id=1, replica_groups=mesh['atoms'=8,'bands'=4] {'bands'}, dimensions={0}, use_global_device_ids=true | all-gather | bytes 983040 | tf_op jit(solution)/shard_map/all_gather | solution.py:88
  186.2 11.8 %psum.30 = f32[128]{0:T(128)S(1)} all-reduce(f32[128]{0:T(128)S(1)} %get-tuple-element.26), channel_id=1, replica_groups=mesh['atoms'=8,'bands'=4] {'atoms'}, use_global_device_ids=true, to_apply=%region_9.10 | all-reduce | flops 128 | bytes 1024 | tf_op jit(solution)/shard_map/psum | solution.py:92
  198.1 17.6 %all_gather.15 = bf16[512,768]{0,1:T(8,128)(2,1)S(1)} all-gather(bf16[128,768]{0,1:T(8,128)(2,1)S(1)} %fusion.55), channel_id=1, replica_groups=mesh['atoms'=8,'bands'=4] {'bands'}, dimensions={0}, use_global_device_ids=true | all-gather | bytes 983040 | tf_op jit(solution)/shard_map/all_gather | solution.py:88
  216.0 11.8 %psum.31 = f32[128]{0:T(128)S(1)} all-reduce(f32[128]{0:T(128)S(1)} %get-tuple-element.28), channel_id=1, replica_groups=mesh['atoms'=8,'bands'=4] {'atoms'}, use_global_device_ids=true, to_apply=%region_11.12 | all-reduce | flops 128 | bytes 1024 | tf_op jit(solution)/shard_map/psum | solution.py:92
  227.9 0.9 copy.72
  (106 shorter events, 27.1 us)
Async XLA Ops:
  0.0 23.2 %collective-permute-start.2 = (bf16[128,768]{1,0:T(8,128)(2,1)}, bf16[128,768]{1,0:T(8,128)(2,1)}, u32[]{:S(2)}, u32[]{:S(2)}) collective-permute-start(bf16[128,768]{1,0:T(8,128)(2,1)} %param.6), channel_id=1, source_target_pairs={{0,8},{4,12},{8,0},{12,4},{16,24},{20,28},{24,16},{28,20},{1,9},{5... | collective-permute-start | bytes 589832 | tf_op jit(solution)/shard_map/ppermute | solution.py:17
  2.9 21.7 %collective-permute-start = (bf16[128,768]{1,0:T(8,128)(2,1)}, bf16[128,768]{1,0:T(8,128)(2,1)}, u32[]{:S(2)}, u32[]{:S(2)}) collective-permute-start(bf16[128,768]{1,0:T(8,128)(2,1)} %param.6), channel_id=1, source_target_pairs={{0,4},{4,0},{8,12},{12,8},{16,20},{20,16},{24,28},{28,24},{1,5},{5... | collective-permute-start | bytes 589832 | tf_op jit(solution)/shard_map/ppermute | solution.py:17
  5.6 2.7 %copy-start.1 = (bf16[128,768]{1,0:T(8,128)(2,1)S(1)}, bf16[128,768]{1,0:T(8,128)(2,1)}, u32[]{:S(2)}) copy-start(bf16[128,768]{1,0:T(8,128)(2,1)} %param.6) | copy-start | bytes 589828
  5.7 4.9 %copy-start.3 = (bf16[2,768,768]{2,1,0:T(8,128)(2,1)S(1)}, bf16[2,768,768]{2,1,0:T(8,128)(2,1)}, u32[]{:S(2)}) copy-start(bf16[2,768,768]{2,1,0:T(8,128)(2,1)} %param.8) | copy-start | bytes 7077892
  8.4 1.7 copy-start.6
  9.6 15.1 %collective-permute-start.1 = (bf16[128,768]{0,1:T(8,128)(2,1)}, bf16[128,768]{0,1:T(8,128)(2,1)}, u32[]{:S(2)}, u32[]{:S(2)}) collective-permute-start(bf16[128,768]{0,1:T(8,128)(2,1)} %fusion.51), channel_id=1, source_target_pairs={{0,4},{4,0},{8,12},{12,8},{16,20},{20,16},{24,28},{28,24},{1,5},{5... | collective-permute-start | bytes 589832 | tf_op jit(solution)/shard_map/ppermute | solution.py:17
  11.8 3.1 %copy-start = (bf16[768,768]{1,0:T(8,128)(2,1)S(1)}, bf16[768,768]{1,0:T(8,128)(2,1)}, u32[]{:S(2)}) copy-start(bf16[768,768]{1,0:T(8,128)(2,1)} %param.7) | copy-start | bytes 3538948
  13.0 11.6 %collective-permute-start.3 = (bf16[128,768]{0,1:T(8,128)(2,1)}, bf16[128,768]{0,1:T(8,128)(2,1)}, u32[]{:S(2)}, u32[]{:S(2)}) collective-permute-start(bf16[128,768]{0,1:T(8,128)(2,1)} %fusion.52), channel_id=1, source_target_pairs={{0,8},{4,12},{8,0},{12,4},{16,24},{20,28},{24,16},{28,20},{1,9},{5... | collective-permute-start | bytes 589832 | tf_op jit(solution)/shard_map/ppermute | solution.py:17
  19.9 2.7 %copy-start.2 = (bf16[128,768]{1,0:T(8,128)(2,1)S(1)}, bf16[128,768]{1,0:T(8,128)(2,1)}, u32[]{:S(2)}) copy-start(bf16[128,768]{1,0:T(8,128)(2,1)} %param.6) | copy-start | bytes 589828
  23.2 1.5 copy-start.4
  26.9 7.7 %collective-permute-start.6 = (bf16[128,768]{0,1:T(8,128)(2,1)S(1)}, bf16[128,768]{0,1:T(8,128)(2,1)S(1)}, u32[]{:S(2)}, u32[]{:S(2)}) collective-permute-start(bf16[128,768]{0,1:T(8,128)(2,1)S(1)} %get-tuple-element.8), channel_id=1, source_target_pairs={{0,8},{4,12},{8,0},{12,4},{16,24},{20,28},{24,16},{28,20},{1,9},{5... | collective-permute-start | bytes 589832 | tf_op jit(solution)/shard_map/ppermute | solution.py:17
  29.6 8.4 %collective-permute-start.4 = (bf16[128,768]{0,1:T(8,128)(2,1)S(1)}, bf16[128,768]{0,1:T(8,128)(2,1)S(1)}, u32[]{:S(2)}, u32[]{:S(2)}) collective-permute-start(bf16[128,768]{0,1:T(8,128)(2,1)S(1)} %get-tuple-element.8), channel_id=1, source_target_pairs={{0,4},{4,0},{8,12},{12,8},{16,20},{20,16},{24,28},{28,24},{1,5},{5... | collective-permute-start | bytes 589832 | tf_op jit(solution)/shard_map/ppermute | solution.py:17
  29.6 5.5 %collective-permute-start.5 = (bf16[128,768]{0,1:T(8,128)(2,1)S(1)}, bf16[128,768]{0,1:T(8,128)(2,1)S(1)}, u32[]{:S(2)}, u32[]{:S(2)}) collective-permute-start(bf16[128,768]{0,1:T(8,128)(2,1)S(1)} %convolution_convert_fusion.13), channel_id=1, source_target_pairs={{0,4},{4,0},{8,12},{12,8},{16,20},{20,16},{24,28},{28,24},{1,5},{5... | collective-permute-start | bytes 589832 | tf_op jit(solution)/shard_map/ppermute | solution.py:17
  30.1 7.8 %collective-permute-start.7 = (bf16[128,768]{0,1:T(8,128)(2,1)S(1)}, bf16[128,768]{0,1:T(8,128)(2,1)S(1)}, u32[]{:S(2)}, u32[]{:S(2)}) collective-permute-start(bf16[128,768]{0,1:T(8,128)(2,1)S(1)} %convolution_convert_fusion.12), channel_id=1, source_target_pairs={{0,8},{4,12},{8,0},{12,4},{16,24},{20,28},{24,16},{28,20},{1,9},{5... | collective-permute-start | bytes 589832 | tf_op jit(solution)/shard_map/ppermute | solution.py:17
  39.0 6.6 %collective-permute-start.10 = (bf16[128,768]{0,1:T(8,128)(2,1)S(1)}, bf16[128,768]{0,1:T(8,128)(2,1)S(1)}, u32[]{:S(2)}, u32[]{:S(2)}) collective-permute-start(bf16[128,768]{0,1:T(8,128)(2,1)S(1)} %get-tuple-element.10), channel_id=1, source_target_pairs={{0,8},{4,12},{8,0},{12,4},{16,24},{20,28},{24,16},{28,20},{1,9},{5... | collective-permute-start | bytes 589832 | tf_op jit(solution)/shard_map/ppermute | solution.py:17
  41.4 7.9 %collective-permute-start.8 = (bf16[128,768]{0,1:T(8,128)(2,1)S(1)}, bf16[128,768]{0,1:T(8,128)(2,1)S(1)}, u32[]{:S(2)}, u32[]{:S(2)}) collective-permute-start(bf16[128,768]{0,1:T(8,128)(2,1)S(1)} %get-tuple-element.10), channel_id=1, source_target_pairs={{0,4},{4,0},{8,12},{12,8},{16,20},{20,16},{24,28},{28,24},{1,5},{5... | collective-permute-start | bytes 589832 | tf_op jit(solution)/shard_map/ppermute | solution.py:17
  41.5 4.6 %collective-permute-start.9 = (bf16[128,768]{0,1:T(8,128)(2,1)S(1)}, bf16[128,768]{0,1:T(8,128)(2,1)S(1)}, u32[]{:S(2)}, u32[]{:S(2)}) collective-permute-start(bf16[128,768]{0,1:T(8,128)(2,1)S(1)} %convolution_convert_fusion.11), channel_id=1, source_target_pairs={{0,4},{4,0},{8,12},{12,8},{16,20},{20,16},{24,28},{28,24},{1,5},{5... | collective-permute-start | bytes 589832 | tf_op jit(solution)/shard_map/ppermute | solution.py:17
  42.0 7.4 %collective-permute-start.11 = (bf16[128,768]{0,1:T(8,128)(2,1)S(1)}, bf16[128,768]{0,1:T(8,128)(2,1)S(1)}, u32[]{:S(2)}, u32[]{:S(2)}) collective-permute-start(bf16[128,768]{0,1:T(8,128)(2,1)S(1)} %convolution_convert_fusion.10), channel_id=1, source_target_pairs={{0,8},{4,12},{8,0},{12,4},{16,24},{20,28},{24,16},{28,20},{1,9},{5... | collective-permute-start | bytes 589832 | tf_op jit(solution)/shard_map/ppermute | solution.py:17
  50.5 7.9 %collective-permute-start.14 = (bf16[128,768]{0,1:T(8,128)(2,1)S(1)}, bf16[128,768]{0,1:T(8,128)(2,1)S(1)}, u32[]{:S(2)}, u32[]{:S(2)}) collective-permute-start(bf16[128,768]{0,1:T(8,128)(2,1)S(1)} %get-tuple-element.12), channel_id=1, source_target_pairs={{0,8},{4,12},{8,0},{12,4},{16,24},{20,28},{24,16},{28,20},{1,9},{5... | collective-permute-start | bytes 589832 | tf_op jit(solution)/shard_map/ppermute | solution.py:17
  52.5 8.8 %collective-permute-start.12 = (bf16[128,768]{0,1:T(8,128)(2,1)S(1)}, bf16[128,768]{0,1:T(8,128)(2,1)S(1)}, u32[]{:S(2)}, u32[]{:S(2)}) collective-permute-start(bf16[128,768]{0,1:T(8,128)(2,1)S(1)} %get-tuple-element.12), channel_id=1, source_target_pairs={{0,4},{4,0},{8,12},{12,8},{16,20},{20,16},{24,28},{28,24},{1,5},{5... | collective-permute-start | bytes 589832 | tf_op jit(solution)/shard_map/ppermute | solution.py:17
  52.6 6.3 %collective-permute-start.13 = (bf16[128,768]{0,1:T(8,128)(2,1)S(1)}, bf16[128,768]{0,1:T(8,128)(2,1)S(1)}, u32[]{:S(2)}, u32[]{:S(2)}) collective-permute-start(bf16[128,768]{0,1:T(8,128)(2,1)S(1)} %convolution_convert_fusion.9), channel_id=1, source_target_pairs={{0,4},{4,0},{8,12},{12,8},{16,20},{20,16},{24,28},{28,24},{1,5},{5... | collective-permute-start | bytes 589832 | tf_op jit(solution)/shard_map/ppermute | solution.py:17
  53.1 8.2 %collective-permute-start.15 = (bf16[128,768]{0,1:T(8,128)(2,1)S(1)}, bf16[128,768]{0,1:T(8,128)(2,1)S(1)}, u32[]{:S(2)}, u32[]{:S(2)}) collective-permute-start(bf16[128,768]{0,1:T(8,128)(2,1)S(1)} %convolution_convert_fusion.8), channel_id=1, source_target_pairs={{0,8},{4,12},{8,0},{12,4},{16,24},{20,28},{24,16},{28,20},{1,9},{5... | collective-permute-start | bytes 589832 | tf_op jit(solution)/shard_map/ppermute | solution.py:17
  62.3 7.1 %collective-permute-start.18 = (bf16[128,768]{0,1:T(8,128)(2,1)S(1)}, bf16[128,768]{0,1:T(8,128)(2,1)S(1)}, u32[]{:S(2)}, u32[]{:S(2)}) collective-permute-start(bf16[128,768]{0,1:T(8,128)(2,1)S(1)} %get-tuple-element.14), channel_id=1, source_target_pairs={{0,8},{4,12},{8,0},{12,4},{16,24},{20,28},{24,16},{28,20},{1,9},{5... | collective-permute-start | bytes 589832 | tf_op jit(solution)/shard_map/ppermute | solution.py:17
  63.5 8.8 %collective-permute-start.16 = (bf16[128,768]{0,1:T(8,128)(2,1)S(1)}, bf16[128,768]{0,1:T(8,128)(2,1)S(1)}, u32[]{:S(2)}, u32[]{:S(2)}) collective-permute-start(bf16[128,768]{0,1:T(8,128)(2,1)S(1)} %get-tuple-element.14), channel_id=1, source_target_pairs={{0,4},{4,0},{8,12},{12,8},{16,20},{20,16},{24,28},{28,24},{1,5},{5... | collective-permute-start | bytes 589832 | tf_op jit(solution)/shard_map/ppermute | solution.py:17
  63.6 6.3 %collective-permute-start.17 = (bf16[128,768]{0,1:T(8,128)(2,1)S(1)}, bf16[128,768]{0,1:T(8,128)(2,1)S(1)}, u32[]{:S(2)}, u32[]{:S(2)}) collective-permute-start(bf16[128,768]{0,1:T(8,128)(2,1)S(1)} %convolution_convert_fusion.7), channel_id=1, source_target_pairs={{0,4},{4,0},{8,12},{12,8},{16,20},{20,16},{24,28},{28,24},{1,5},{5... | collective-permute-start | bytes 589832 | tf_op jit(solution)/shard_map/ppermute | solution.py:17
  64.1 8.2 %collective-permute-start.19 = (bf16[128,768]{0,1:T(8,128)(2,1)S(1)}, bf16[128,768]{0,1:T(8,128)(2,1)S(1)}, u32[]{:S(2)}, u32[]{:S(2)}) collective-permute-start(bf16[128,768]{0,1:T(8,128)(2,1)S(1)} %convolution_convert_fusion.6), channel_id=1, source_target_pairs={{0,8},{4,12},{8,0},{12,4},{16,24},{20,28},{24,16},{28,20},{1,9},{5... | collective-permute-start | bytes 589832 | tf_op jit(solution)/shard_map/ppermute | solution.py:17
  73.4 7.0 %collective-permute-start.22 = (bf16[128,768]{0,1:T(8,128)(2,1)S(1)}, bf16[128,768]{0,1:T(8,128)(2,1)S(1)}, u32[]{:S(2)}, u32[]{:S(2)}) collective-permute-start(bf16[128,768]{0,1:T(8,128)(2,1)S(1)} %get-tuple-element.16), channel_id=1, source_target_pairs={{0,8},{4,12},{8,0},{12,4},{16,24},{20,28},{24,16},{28,20},{1,9},{5... | collective-permute-start | bytes 589832 | tf_op jit(solution)/shard_map/ppermute | solution.py:17
  74.6 8.7 %collective-permute-start.20 = (bf16[128,768]{0,1:T(8,128)(2,1)S(1)}, bf16[128,768]{0,1:T(8,128)(2,1)S(1)}, u32[]{:S(2)}, u32[]{:S(2)}) collective-permute-start(bf16[128,768]{0,1:T(8,128)(2,1)S(1)} %get-tuple-element.16), channel_id=1, source_target_pairs={{0,4},{4,0},{8,12},{12,8},{16,20},{20,16},{24,28},{28,24},{1,5},{5... | collective-permute-start | bytes 589832 | tf_op jit(solution)/shard_map/ppermute | solution.py:17
  74.7 6.1 %collective-permute-start.21 = (bf16[128,768]{0,1:T(8,128)(2,1)S(1)}, bf16[128,768]{0,1:T(8,128)(2,1)S(1)}, u32[]{:S(2)}, u32[]{:S(2)}) collective-permute-start(bf16[128,768]{0,1:T(8,128)(2,1)S(1)} %convolution_convert_fusion.5), channel_id=1, source_target_pairs={{0,4},{4,0},{8,12},{12,8},{16,20},{20,16},{24,28},{28,24},{1,5},{5... | collective-permute-start | bytes 589832 | tf_op jit(solution)/shard_map/ppermute | solution.py:17
  75.2 8.1 %collective-permute-start.23 = (bf16[128,768]{0,1:T(8,128)(2,1)S(1)}, bf16[128,768]{0,1:T(8,128)(2,1)S(1)}, u32[]{:S(2)}, u32[]{:S(2)}) collective-permute-start(bf16[128,768]{0,1:T(8,128)(2,1)S(1)} %convolution_convert_fusion.4), channel_id=1, source_target_pairs={{0,8},{4,12},{8,0},{12,4},{16,24},{20,28},{24,16},{28,20},{1,9},{5... | collective-permute-start | bytes 589832 | tf_op jit(solution)/shard_map/ppermute | solution.py:17
  84.4 6.1 %collective-permute-start.26 = (bf16[128,768]{0,1:T(8,128)(2,1)S(1)}, bf16[128,768]{0,1:T(8,128)(2,1)S(1)}, u32[]{:S(2)}, u32[]{:S(2)}) collective-permute-start(bf16[128,768]{0,1:T(8,128)(2,1)S(1)} %get-tuple-element.18), channel_id=1, source_target_pairs={{0,8},{4,12},{8,0},{12,4},{16,24},{20,28},{24,16},{28,20},{1,9},{5... | collective-permute-start | bytes 589832 | tf_op jit(solution)/shard_map/ppermute | solution.py:17
  86.4 7.9 %collective-permute-start.24 = (bf16[128,768]{0,1:T(8,128)(2,1)S(1)}, bf16[128,768]{0,1:T(8,128)(2,1)S(1)}, u32[]{:S(2)}, u32[]{:S(2)}) collective-permute-start(bf16[128,768]{0,1:T(8,128)(2,1)S(1)} %get-tuple-element.18), channel_id=1, source_target_pairs={{0,4},{4,0},{8,12},{12,8},{16,20},{20,16},{24,28},{28,24},{1,5},{5... | collective-permute-start | bytes 589832 | tf_op jit(solution)/shard_map/ppermute | solution.py:17
  86.5 4.5 %collective-permute-start.25 = (bf16[128,768]{0,1:T(8,128)(2,1)S(1)}, bf16[128,768]{0,1:T(8,128)(2,1)S(1)}, u32[]{:S(2)}, u32[]{:S(2)}) collective-permute-start(bf16[128,768]{0,1:T(8,128)(2,1)S(1)} %convolution_convert_fusion.3), channel_id=1, source_target_pairs={{0,4},{4,0},{8,12},{12,8},{16,20},{20,16},{24,28},{28,24},{1,5},{5... | collective-permute-start | bytes 589832 | tf_op jit(solution)/shard_map/ppermute | solution.py:17
  87.0 7.3 %collective-permute-start.27 = (bf16[128,768]{0,1:T(8,128)(2,1)S(1)}, bf16[128,768]{0,1:T(8,128)(2,1)S(1)}, u32[]{:S(2)}, u32[]{:S(2)}) collective-permute-start(bf16[128,768]{0,1:T(8,128)(2,1)S(1)} %convolution_convert_fusion.2), channel_id=1, source_target_pairs={{0,8},{4,12},{8,0},{12,4},{16,24},{20,28},{24,16},{28,20},{1,9},{5... | collective-permute-start | bytes 589832 | tf_op jit(solution)/shard_map/ppermute | solution.py:17
  96.0 7.9 %collective-permute-start.30 = (bf16[128,768]{0,1:T(8,128)(2,1)S(1)}, bf16[128,768]{0,1:T(8,128)(2,1)S(1)}, u32[]{:S(2)}, u32[]{:S(2)}) collective-permute-start(bf16[128,768]{0,1:T(8,128)(2,1)S(1)} %get-tuple-element.20), channel_id=1, source_target_pairs={{0,8},{4,12},{8,0},{12,4},{16,24},{20,28},{24,16},{28,20},{1,9},{5... | collective-permute-start | bytes 589832 | tf_op jit(solution)/shard_map/ppermute | solution.py:17
  97.6 9.2 %collective-permute-start.28 = (bf16[128,768]{0,1:T(8,128)(2,1)S(1)}, bf16[128,768]{0,1:T(8,128)(2,1)S(1)}, u32[]{:S(2)}, u32[]{:S(2)}) collective-permute-start(bf16[128,768]{0,1:T(8,128)(2,1)S(1)} %get-tuple-element.20), channel_id=1, source_target_pairs={{0,4},{4,0},{8,12},{12,8},{16,20},{20,16},{24,28},{28,24},{1,5},{5... | collective-permute-start | bytes 589832 | tf_op jit(solution)/shard_map/ppermute | solution.py:17
  97.6 6.8 %collective-permute-start.29 = (bf16[128,768]{0,1:T(8,128)(2,1)S(1)}, bf16[128,768]{0,1:T(8,128)(2,1)S(1)}, u32[]{:S(2)}, u32[]{:S(2)}) collective-permute-start(bf16[128,768]{0,1:T(8,128)(2,1)S(1)} %convolution_convert_fusion.1), channel_id=1, source_target_pairs={{0,4},{4,0},{8,12},{12,8},{16,20},{20,16},{24,28},{28,24},{1,5},{5... | collective-permute-start | bytes 589832 | tf_op jit(solution)/shard_map/ppermute | solution.py:17
  98.1 8.7 %collective-permute-start.31 = (bf16[128,768]{0,1:T(8,128)(2,1)S(1)}, bf16[128,768]{0,1:T(8,128)(2,1)S(1)}, u32[]{:S(2)}, u32[]{:S(2)}) collective-permute-start(bf16[128,768]{0,1:T(8,128)(2,1)S(1)} %convolution_convert_fusion), channel_id=1, source_target_pairs={{0,8},{4,12},{8,0},{12,4},{16,24},{20,28},{24,16},{28,20},{1,9},{5... | collective-permute-start | bytes 589832 | tf_op jit(solution)/shard_map/ppermute | solution.py:17
  106.8 19.4 %copy-start.5 = (bf16[4,512,128]{2,1,0:T(8,128)(2,1)S(1)}, bf16[4,512,128]{2,1,0:T(8,128)(2,1)}, u32[]{:S(2)}) copy-start(bf16[4,512,128]{2,1,0:T(8,128)(2,1)} %param.11) | copy-start | bytes 1572868
where the time goes:
time: 229 us
  blocking collectives  119 us (52%)
  waiting for transfers between devices  42.9 us (19%)
  matrix products  32.2 us (14%)
  starting transfers between devices  22 us (10%)
  local copies, waits for them, and re-layouts  6.76 us (3%)
  other arithmetic  5.57 us (2%)
    all_gather x4, blocking collectives, body(): lax.all_gather(rounded, 'bands', axis=0, tiled=True)  71.6 us
    psum x4, blocking collectives, body(): squares = lax.psum(jnp.sum(mixed_rows * mixed_rows, axis=1), 'atoms')  47.2 us
    ppermute x32, waiting for transfers between devices, swapped(): return lax.ppermute(value, axis, pairs)  42.9 us
    ppermute x32, starting transfers between devices, swapped(): return lax.ppermute(value, axis, pairs)  22 us
    dot_general x16, matrix products, apply_operator(): sent_term = jnp.dot(values, pair_mat, preferred_element_type=jnp.float32)  10.7 us
    dot_general x16, matrix products, apply_operator(): lax.dot_general(other_rows, pair_mat, (((1,), (1,)), ((), ())), preferred...  9.66 us
    dot_general x8, matrix products, apply_operator(): result = jnp.dot(values, diag_sym, preferred_element_type=jnp.float32)  4.85 us
  transfers between devices with their start and end apart: 32, of which 14 were waited for; matrix products, arithmetic and copies ran while one was open for 14% of the time, Pallas kernels for 0%

commit v1 on v0

--- a/solution.py
+++ b/solution.py
@@ -89,7 +89,7 @@
             (((0,), (0,)), ((), ())),
             preferred_element_type=jnp.float32,
         )
-        squares = lax.psum(jnp.sum(mixed_rows * mixed_rows, axis=1), "atoms")
+        squares = jnp.sum(lax.all_gather(jnp.sum(mixed_rows * mixed_rows, axis=1), "atoms"), axis=0)
         col_norm = jnp.sqrt(squares / total_orbitals + norm_eps)
         basis_rows = mixed_rows / col_norm[:, None]
     return basis_rows

time: 229 us -> 216 us (0.943)
  blocking collectives: 119 us -> 106 us
    psum x4 -> x0, blocking collectives: 47.2 us -> none  [body(): squares = lax.psum(jnp.sum(mixed_rows * mixed_rows, axis=1), 'atoms')]
    all_gather x0 -> x4, blocking collectives: none -> 33 us  [body(): lax.all_gather(jnp.sum(mixed_rows * mixed_rows, axis=1), 'atoms')]
  transfers between devices with their start and end apart: 32 -> 32, of which waited for: 14 -> 14; matrix products, arithmetic and copies ran while one was open for 14% -> 15% of each run, Pallas kernels for 0% -> 0%
where the time goes in v1:
time: 216 us
  blocking collectives  106 us (49%)
  waiting for transfers between devices  42.9 us (20%)
  matrix products  31.7 us (15%)
  starting transfers between devices  22 us (10%)
  local copies, waits for them, and re-layouts  6.76 us (3%)
  other arithmetic  5.68 us (3%)
    all_gather x4, blocking collectives, body(): lax.all_gather(rounded, 'bands', axis=0, tiled=True)  73 us
    ppermute x32, waiting for transfers between devices, swapped(): return lax.ppermute(value, axis, pairs)  42.9 us
    all_gather x4, blocking collectives, body(): lax.all_gather(jnp.sum(mixed_rows * mixed_rows, axis=1), 'atoms')  33 us
    ppermute x32, starting transfers between devices, swapped(): return lax.ppermute(value, axis, pairs)  22 us
    dot_general x16, matrix products, apply_operator(): sent_term = jnp.dot(values, pair_mat, preferred_element_type=jnp.float32)  10.7 us
    dot_general x16, matrix products, apply_operator(): lax.dot_general(other_rows, pair_mat, (((1,), (1,)), ((), ())), preferred...  9.66 us
    dot_general x8, matrix products, apply_operator(): result = jnp.dot(values, diag_sym, preferred_element_type=jnp.float32)  4.84 us
  transfers between devices with their start and end apart: 32, of which 14 were waited for; matrix products, arithmetic and copies ran while one was open for 15% of the time, Pallas kernels for 0%

profile of v1, /device:TPU:0, one launch (start us, length us, event | category | flops | bytes accessed | tf_op | source)
XLA Modules:
  0.0 215.5 jit_solution(8909072356684999018)
XLA Ops:
  0.0 2.9 %collective-permute-start.2 = (bf16[128,768]{1,0:T(8,128)(2,1)}, bf16[128,768]{1,0:T(8,128)(2,1)}, u32[]{:S(2)}, u32[]{:S(2)}) collective-permute-start(bf16[128,768]{1,0:T(8,128)(2,1)} %param.6), channel_id=1, source_target_pairs={{0,8},{4,12},{8,0},{12,4},{16,24},{20,28},{24,16},{28,20},{1,9},{5... | collective-permute-start | bytes 589832 | tf_op jit(solution)/shard_map/ppermute | solution.py:17
  2.9 1.0 dynamic-slice_reduce_fusion.1
  4.5 0.9 fusion.70
  5.4 2.7 %fusion.1 = bf16[768,768]{1,0:T(8,128)(2,1)S(1)} fusion(f32[768,4]{0,1:T(4,128)S(1)} %fusion.70, bf16[2,768,768]{2,1,0:T(8,128)(2,1)} %param.8, s32[4]{0:T(128)S(1)} %bitcast.159, s32[4]{0:T(128)S(1)} %bitcast_subtract_fusion.2), kind=kOutput, calls=%fused_computation.3 | convolution fusion | flops 30090240 | bytes 2371616 | tf_op jit(solution)/shard_map/dot_general | solution.py:68
  8.1 1.2 fusion.51
  10.0 1.2 fusion
  11.3 1.2 fusion.52
  12.6 1.7 copy.74
  14.3 2.0 add_multiply_fusion
  16.3 3.1 %copy.73 = f32[768,768]{0,1:T(8,128)} copy(f32[768,768]{1,0:T(8,128)} %add_multiply_fusion) | data formatting | bytes 4718592 | tf_op jit(solution)/shard_map/mul | solution.py:58
  19.4 2.7 %fusion.2 = bf16[768,768]{1,0:T(8,128)(2,1)S(1)} fusion(f32[768,768]{0,1:T(8,128)} %copy.73, f32[768]{0:T(1024)S(1)} %select_reduce_fusion, bf16[768,768]{1,0:T(8,128)(2,1)} %param.7), kind=kLoop, calls=%fused_computation.5 | loop fusion | flops 5308416 | bytes 4721664 | tf_op jit(solution)/shard_map/convert_element_type | solution.py:59
  22.7 1.4 convolution_bitcast_fusion
  24.1 1.6 multiply_convert_fusion
  26.3 2.1 collective-permute-start.6
  30.2 3.9 %collective-permute-done.6 = bf16[128,768]{0,1:T(8,128)(2,1)S(1)} collective-permute-done((bf16[128,768]{0,1:T(8,128)(2,1)S(1)}, bf16[128,768]{0,1:T(8,128)(2,1)S(1)}, u32[]{:S(2)}, u32[]{:S(2)}) %collective-permute-start.6) | collective-permute-done | bytes 196640 | tf_op jit(solution)/shard_map/ppermute | solution.py:17
  34.6 2.8 %collective-permute-done.7 = bf16[128,768]{0,1:T(8,128)(2,1)S(1)} collective-permute-done((bf16[128,768]{0,1:T(8,128)(2,1)S(1)}, bf16[128,768]{0,1:T(8,128)(2,1)S(1)}, u32[]{:S(2)}, u32[]{:S(2)}) %collective-permute-start.7) | collective-permute-done | bytes 196640 | tf_op jit(solution)/shard_map/ppermute | solution.py:17
  38.5 1.8 collective-permute-start.10
  42.4 2.7 %collective-permute-done.10 = bf16[128,768]{0,1:T(8,128)(2,1)S(1)} collective-permute-done((bf16[128,768]{0,1:T(8,128)(2,1)S(1)}, bf16[128,768]{0,1:T(8,128)(2,1)S(1)}, u32[]{:S(2)}, u32[]{:S(2)}) %collective-permute-start.10) | collective-permute-done | bytes 196640 | tf_op jit(solution)/shard_map/ppermute | solution.py:17
  45.6 3.2 %collective-permute-done.11 = bf16[128,768]{0,1:T(8,128)(2,1)S(1)} collective-permute-done((bf16[128,768]{0,1:T(8,128)(2,1)S(1)}, bf16[128,768]{0,1:T(8,128)(2,1)S(1)}, u32[]{:S(2)}, u32[]{:S(2)}) %collective-permute-start.11) | collective-permute-done | bytes 196640 | tf_op jit(solution)/shard_map/ppermute | solution.py:17
  49.9 1.4 collective-permute-start.14
  52.5 0.6 collective-permute-start.15
  53.8 3.9 %collective-permute-done.14 = bf16[128,768]{0,1:T(8,128)(2,1)S(1)} collective-permute-done((bf16[128,768]{0,1:T(8,128)(2,1)S(1)}, bf16[128,768]{0,1:T(8,128)(2,1)S(1)}, u32[]{:S(2)}, u32[]{:S(2)}) %collective-permute-start.14) | collective-permute-done | bytes 196640 | tf_op jit(solution)/shard_map/ppermute | solution.py:17
  58.1 2.5 %collective-permute-done.15 = bf16[128,768]{0,1:T(8,128)(2,1)S(1)} collective-permute-done((bf16[128,768]{0,1:T(8,128)(2,1)S(1)}, bf16[128,768]{0,1:T(8,128)(2,1)S(1)}, u32[]{:S(2)}, u32[]{:S(2)}) %collective-permute-start.15) | collective-permute-done | bytes 196640 | tf_op jit(solution)/shard_map/ppermute | solution.py:17
  61.8 0.6 collective-permute-start.18
  63.6 1.5 collective-permute-start.19
  65.0 0.8 fusion.97
  65.8 3.0 %collective-permute-done.18 = bf16[128,768]{0,1:T(8,128)(2,1)S(1)} collective-permute-done((bf16[128,768]{0,1:T(8,128)(2,1)S(1)}, bf16[128,768]{0,1:T(8,128)(2,1)S(1)}, u32[]{:S(2)}, u32[]{:S(2)}) %collective-permute-start.18) | collective-permute-done | bytes 196640 | tf_op jit(solution)/shard_map/ppermute | solution.py:17
  69.4 2.4 %collective-permute-done.19 = bf16[128,768]{0,1:T(8,128)(2,1)S(1)} collective-permute-done((bf16[128,768]{0,1:T(8,128)(2,1)S(1)}, bf16[128,768]{0,1:T(8,128)(2,1)S(1)}, u32[]{:S(2)}, u32[]{:S(2)}) %collective-permute-start.19) | collective-permute-done | bytes 196640 | tf_op jit(solution)/shard_map/ppermute | solution.py:17
  72.8 0.6 collective-permute-start.22
  74.6 1.5 collective-permute-start.23
  76.7 3.2 %collective-permute-done.22 = bf16[128,768]{0,1:T(8,128)(2,1)S(1)} collective-permute-done((bf16[128,768]{0,1:T(8,128)(2,1)S(1)}, bf16[128,768]{0,1:T(8,128)(2,1)S(1)}, u32[]{:S(2)}, u32[]{:S(2)}) %collective-permute-start.22) | collective-permute-done | bytes 196640 | tf_op jit(solution)/shard_map/ppermute | solution.py:17
  80.3 2.4 %collective-permute-done.23 = bf16[128,768]{0,1:T(8,128)(2,1)S(1)} collective-permute-done((bf16[128,768]{0,1:T(8,128)(2,1)S(1)}, bf16[128,768]{0,1:T(8,128)(2,1)S(1)}, u32[]{:S(2)}, u32[]{:S(2)}) %collective-permute-start.23) | collective-permute-done | bytes 196640 | tf_op jit(solution)/shard_map/ppermute | solution.py:17
  83.9 1.4 collective-permute-start.26
  86.5 0.7 collective-permute-start.27
  87.7 2.3 %collective-permute-done.26 = bf16[128,768]{0,1:T(8,128)(2,1)S(1)} collective-permute-done((bf16[128,768]{0,1:T(8,128)(2,1)S(1)}, bf16[128,768]{0,1:T(8,128)(2,1)S(1)}, u32[]{:S(2)}, u32[]{:S(2)}) %collective-permute-start.26) | collective-permute-done | bytes 196640 | tf_op jit(solution)/shard_map/ppermute | solution.py:17
  90.5 3.3 %collective-permute-done.27 = bf16[128,768]{0,1:T(8,128)(2,1)S(1)} collective-permute-done((bf16[128,768]{0,1:T(8,128)(2,1)S(1)}, bf16[128,768]{0,1:T(8,128)(2,1)S(1)}, u32[]{:S(2)}, u32[]{:S(2)}) %collective-permute-start.27) | collective-permute-done | bytes 196640 | tf_op jit(solution)/shard_map/ppermute | solution.py:17
  95.5 1.6 collective-permute-start.30
  98.7 4.7 %collective-permute-done.30 = bf16[128,768]{0,1:T(8,128)(2,1)S(1)} collective-permute-done((bf16[128,768]{0,1:T(8,128)(2,1)S(1)}, bf16[128,768]{0,1:T(8,128)(2,1)S(1)}, u32[]{:S(2)}, u32[]{:S(2)}) %collective-permute-start.30) | collective-permute-done | bytes 196640 | tf_op jit(solution)/shard_map/ppermute | solution.py:17
  103.9 2.4 %collective-permute-done.31 = bf16[128,768]{0,1:T(8,128)(2,1)S(1)} collective-permute-done((bf16[128,768]{0,1:T(8,128)(2,1)S(1)}, bf16[128,768]{0,1:T(8,128)(2,1)S(1)}, u32[]{:S(2)}, u32[]{:S(2)}) %collective-permute-start.31) | collective-permute-done | bytes 196640 | tf_op jit(solution)/shard_map/ppermute | solution.py:17
  106.8 18.9 %all_gather.36 = bf16[512,768]{0,1:T(8,128)(2,1)S(1)} all-gather(bf16[128,768]{0,1:T(8,128)(2,1)S(1)} %fusion.50), channel_id=1, replica_groups=mesh['atoms'=8,'bands'=4] {'bands'}, dimensions={0}, use_global_device_ids=true | all-gather | bytes 983040 | tf_op jit(solution)/shard_map/all_gather | solution.py:88
  126.1 8.8 %all-gather.4 = f32[8,1,128]{2,1,0:T(1,128)S(1)} all-gather(f32[1,1,128]{2,1,0:T(1,128)S(1)} %bitcast.162), channel_id=2, replica_groups=mesh['atoms'=8,'bands'=4] {'atoms'}, dimensions={0}, use_global_device_ids=true | all-gather | bytes 4608 | tf_op jit(solution)/shard_map/all_gather | solution.py:92
  134.9 18.0 %all_gather.39 = bf16[512,768]{0,1:T(8,128)(2,1)S(1)} all-gather(bf16[128,768]{0,1:T(8,128)(2,1)S(1)} %fusion.53), channel_id=1, replica_groups=mesh['atoms'=8,'bands'=4] {'bands'}, dimensions={0}, use_global_device_ids=true | all-gather | bytes 983040 | tf_op jit(solution)/shard_map/all_gather | solution.py:88
  153.3 7.7 %all-gather.5 = f32[8,1,128]{2,1,0:T(1,128)S(1)} all-gather(f32[1,1,128]{2,1,0:T(1,128)S(1)} %bitcast.163), channel_id=3, replica_groups=mesh['atoms'=8,'bands'=4] {'atoms'}, dimensions={0}, use_global_device_ids=true | all-gather | bytes 4608 | tf_op jit(solution)/shard_map/all_gather | solution.py:92
  161.2 18.0 %all_gather.42 = bf16[512,768]{0,1:T(8,128)(2,1)S(1)} all-gather(bf16[128,768]{0,1:T(8,128)(2,1)S(1)} %fusion.54), channel_id=1, replica_groups=mesh['atoms'=8,'bands'=4] {'bands'}, dimensions={0}, use_global_device_ids=true | all-gather | bytes 983040 | tf_op jit(solution)/shard_map/all_gather | solution.py:88
  179.5 8.8 %all-gather.6 = f32[8,1,128]{2,1,0:T(1,128)S(1)} all-gather(f32[1,1,128]{2,1,0:T(1,128)S(1)} %bitcast.164), channel_id=4, replica_groups=mesh['atoms'=8,'bands'=4] {'atoms'}, dimensions={0}, use_global_device_ids=true | all-gather | bytes 4608 | tf_op jit(solution)/shard_map/all_gather | solution.py:92
  188.4 18.0 %all_gather.45 = bf16[512,768]{0,1:T(8,128)(2,1)S(1)} all-gather(bf16[128,768]{0,1:T(8,128)(2,1)S(1)} %fusion.55), channel_id=1, replica_groups=mesh['atoms'=8,'bands'=4] {'bands'}, dimensions={0}, use_global_device_ids=true | all-gather | bytes 983040 | tf_op jit(solution)/shard_map/all_gather | solution.py:88
  206.8 7.8 %all-gather.7 = f32[8,1,128]{2,1,0:T(1,128)S(1)} all-gather(f32[1,1,128]{2,1,0:T(1,128)S(1)} %bitcast.165), channel_id=5, replica_groups=mesh['atoms'=8,'bands'=4] {'atoms'}, dimensions={0}, use_global_device_ids=true | all-gather | bytes 4608 | tf_op jit(solution)/shard_map/all_gather | solution.py:92
  214.6 0.9 copy.110
  (110 shorter events, 26.9 us)
Async XLA Ops:
  0.0 22.7 %collective-permute-start.2 = (bf16[128,768]{1,0:T(8,128)(2,1)}, bf16[128,768]{1,0:T(8,128)(2,1)}, u32[]{:S(2)}, u32[]{:S(2)}) collective-permute-start(bf16[128,768]{1,0:T(8,128)(2,1)} %param.6), channel_id=1, source_target_pairs={{0,8},{4,12},{8,0},{12,4},{16,24},{20,28},{24,16},{28,20},{1,9},{5... | collective-permute-start | bytes 589832 | tf_op jit(solution)/shard_map/ppermute | solution.py:17
  2.9 21.2 %collective-permute-start = (bf16[128,768]{1,0:T(8,128)(2,1)}, bf16[128,768]{1,0:T(8,128)(2,1)}, u32[]{:S(2)}, u32[]{:S(2)}) collective-permute-start(bf16[128,768]{1,0:T(8,128)(2,1)} %param.6), channel_id=1, source_target_pairs={{0,4},{4,0},{8,12},{12,8},{16,20},{20,16},{24,28},{28,24},{1,5},{5... | collective-permute-start | bytes 589832 | tf_op jit(solution)/shard_map/ppermute | solution.py:17
  5.4 2.7 %copy-start.1 = (bf16[128,768]{1,0:T(8,128)(2,1)S(1)}, bf16[128,768]{1,0:T(8,128)(2,1)}, u32[]{:S(2)}) copy-start(bf16[128,768]{1,0:T(8,128)(2,1)} %param.6) | copy-start | bytes 589828
  5.4 4.6 %copy-start.3 = (bf16[2,768,768]{2,1,0:T(8,128)(2,1)S(1)}, bf16[2,768,768]{2,1,0:T(8,128)(2,1)}, u32[]{:S(2)}) copy-start(bf16[2,768,768]{2,1,0:T(8,128)(2,1)} %param.8) | copy-start | bytes 7077892
  8.1 1.7 copy-start.6
  9.3 14.8 %collective-permute-start.1 = (bf16[128,768]{0,1:T(8,128)(2,1)}, bf16[128,768]{0,1:T(8,128)(2,1)}, u32[]{:S(2)}, u32[]{:S(2)}) collective-permute-start(bf16[128,768]{0,1:T(8,128)(2,1)} %fusion.51), channel_id=1, source_target_pairs={{0,4},{4,0},{8,12},{12,8},{16,20},{20,16},{24,28},{28,24},{1,5},{5... | collective-permute-start | bytes 589832 | tf_op jit(solution)/shard_map/ppermute | solution.py:17
  11.3 3.1 %copy-start = (bf16[768,768]{1,0:T(8,128)(2,1)S(1)}, bf16[768,768]{1,0:T(8,128)(2,1)}, u32[]{:S(2)}) copy-start(bf16[768,768]{1,0:T(8,128)(2,1)} %param.7) | copy-start | bytes 3538948
  12.5 11.6 %collective-permute-start.3 = (bf16[128,768]{0,1:T(8,128)(2,1)}, bf16[128,768]{0,1:T(8,128)(2,1)}, u32[]{:S(2)}, u32[]{:S(2)}) collective-permute-start(bf16[128,768]{0,1:T(8,128)(2,1)} %fusion.52), channel_id=1, source_target_pairs={{0,8},{4,12},{8,0},{12,4},{16,24},{20,28},{24,16},{28,20},{1,9},{5... | collective-permute-start | bytes 589832 | tf_op jit(solution)/shard_map/ppermute | solution.py:17
  19.4 2.7 %copy-start.2 = (bf16[128,768]{1,0:T(8,128)(2,1)S(1)}, bf16[128,768]{1,0:T(8,128)(2,1)}, u32[]{:S(2)}) copy-start(bf16[128,768]{1,0:T(8,128)(2,1)} %param.6) | copy-start | bytes 589828
  22.6 1.5 copy-start.4
  26.3 7.8 %collective-permute-start.6 = (bf16[128,768]{0,1:T(8,128)(2,1)S(1)}, bf16[128,768]{0,1:T(8,128)(2,1)S(1)}, u32[]{:S(2)}, u32[]{:S(2)}) collective-permute-start(bf16[128,768]{0,1:T(8,128)(2,1)S(1)} %get-tuple-element.8), channel_id=1, source_target_pairs={{0,8},{4,12},{8,0},{12,4},{16,24},{20,28},{24,16},{28,20},{1,9},{5... | collective-permute-start | bytes 589832 | tf_op jit(solution)/shard_map/ppermute | solution.py:17
  29.0 8.4 %collective-permute-start.4 = (bf16[128,768]{0,1:T(8,128)(2,1)S(1)}, bf16[128,768]{0,1:T(8,128)(2,1)S(1)}, u32[]{:S(2)}, u32[]{:S(2)}) collective-permute-start(bf16[128,768]{0,1:T(8,128)(2,1)S(1)} %get-tuple-element.8), channel_id=1, source_target_pairs={{0,4},{4,0},{8,12},{12,8},{16,20},{20,16},{24,28},{28,24},{1,5},{5... | collective-permute-start | bytes 589832 | tf_op jit(solution)/shard_map/ppermute | solution.py:17
  29.1 5.5 %collective-permute-start.5 = (bf16[128,768]{0,1:T(8,128)(2,1)S(1)}, bf16[128,768]{0,1:T(8,128)(2,1)S(1)}, u32[]{:S(2)}, u32[]{:S(2)}) collective-permute-start(bf16[128,768]{0,1:T(8,128)(2,1)S(1)} %convolution_convert_fusion.13), channel_id=1, source_target_pairs={{0,4},{4,0},{8,12},{12,8},{16,20},{20,16},{24,28},{28,24},{1,5},{5... | collective-permute-start | bytes 589832 | tf_op jit(solution)/shard_map/ppermute | solution.py:17
  29.6 7.8 %collective-permute-start.7 = (bf16[128,768]{0,1:T(8,128)(2,1)S(1)}, bf16[128,768]{0,1:T(8,128)(2,1)S(1)}, u32[]{:S(2)}, u32[]{:S(2)}) collective-permute-start(bf16[128,768]{0,1:T(8,128)(2,1)S(1)} %convolution_convert_fusion.12), channel_id=1, source_target_pairs={{0,8},{4,12},{8,0},{12,4},{16,24},{20,28},{24,16},{28,20},{1,9},{5... | collective-permute-start | bytes 589832 | tf_op jit(solution)/shard_map/ppermute | solution.py:17
  38.5 6.6 %collective-permute-start.10 = (bf16[128,768]{0,1:T(8,128)(2,1)S(1)}, bf16[128,768]{0,1:T(8,128)(2,1)S(1)}, u32[]{:S(2)}, u32[]{:S(2)}) collective-permute-start(bf16[128,768]{0,1:T(8,128)(2,1)S(1)} %get-tuple-element.10), channel_id=1, source_target_pairs={{0,8},{4,12},{8,0},{12,4},{16,24},{20,28},{24,16},{28,20},{1,9},{5... | collective-permute-start | bytes 589832 | tf_op jit(solution)/shard_map/ppermute | solution.py:17
  40.9 7.9 %collective-permute-start.8 = (bf16[128,768]{0,1:T(8,128)(2,1)S(1)}, bf16[128,768]{0,1:T(8,128)(2,1)S(1)}, u32[]{:S(2)}, u32[]{:S(2)}) collective-permute-start(bf16[128,768]{0,1:T(8,128)(2,1)S(1)} %get-tuple-element.10), channel_id=1, source_target_pairs={{0,4},{4,0},{8,12},{12,8},{16,20},{20,16},{24,28},{28,24},{1,5},{5... | collective-permute-start | bytes 589832 | tf_op jit(solution)/shard_map/ppermute | solution.py:17
  41.0 4.6 %collective-permute-start.9 = (bf16[128,768]{0,1:T(8,128)(2,1)S(1)}, bf16[128,768]{0,1:T(8,128)(2,1)S(1)}, u32[]{:S(2)}, u32[]{:S(2)}) collective-permute-start(bf16[128,768]{0,1:T(8,128)(2,1)S(1)} %convolution_convert_fusion.11), channel_id=1, source_target_pairs={{0,4},{4,0},{8,12},{12,8},{16,20},{20,16},{24,28},{28,24},{1,5},{5... | collective-permute-start | bytes 589832 | tf_op jit(solution)/shard_map/ppermute | solution.py:17
  41.5 7.3 %collective-permute-start.11 = (bf16[128,768]{0,1:T(8,128)(2,1)S(1)}, bf16[128,768]{0,1:T(8,128)(2,1)S(1)}, u32[]{:S(2)}, u32[]{:S(2)}) collective-permute-start(bf16[128,768]{0,1:T(8,128)(2,1)S(1)} %convolution_convert_fusion.10), channel_id=1, source_target_pairs={{0,8},{4,12},{8,0},{12,4},{16,24},{20,28},{24,16},{28,20},{1,9},{5... | collective-permute-start | bytes 589832 | tf_op jit(solution)/shard_map/ppermute | solution.py:17
  49.9 7.7 %collective-permute-start.14 = (bf16[128,768]{0,1:T(8,128)(2,1)S(1)}, bf16[128,768]{0,1:T(8,128)(2,1)S(1)}, u32[]{:S(2)}, u32[]{:S(2)}) collective-permute-start(bf16[128,768]{0,1:T(8,128)(2,1)S(1)} %get-tuple-element.12), channel_id=1, source_target_pairs={{0,8},{4,12},{8,0},{12,4},{16,24},{20,28},{24,16},{28,20},{1,9},{5... | collective-permute-start | bytes 589832 | tf_op jit(solution)/shard_map/ppermute | solution.py:17
  51.9 8.7 %collective-permute-start.12 = (bf16[128,768]{0,1:T(8,128)(2,1)S(1)}, bf16[128,768]{0,1:T(8,128)(2,1)S(1)}, u32[]{:S(2)}, u32[]{:S(2)}) collective-permute-start(bf16[128,768]{0,1:T(8,128)(2,1)S(1)} %get-tuple-element.12), channel_id=1, source_target_pairs={{0,4},{4,0},{8,12},{12,8},{16,20},{20,16},{24,28},{28,24},{1,5},{5... | collective-permute-start | bytes 589832 | tf_op jit(solution)/shard_map/ppermute | solution.py:17
  52.0 6.1 %collective-permute-start.13 = (bf16[128,768]{0,1:T(8,128)(2,1)S(1)}, bf16[128,768]{0,1:T(8,128)(2,1)S(1)}, u32[]{:S(2)}, u32[]{:S(2)}) collective-permute-start(bf16[128,768]{0,1:T(8,128)(2,1)S(1)} %convolution_convert_fusion.9), channel_id=1, source_target_pairs={{0,4},{4,0},{8,12},{12,8},{16,20},{20,16},{24,28},{28,24},{1,5},{5... | collective-permute-start | bytes 589832 | tf_op jit(solution)/shard_map/ppermute | solution.py:17
  52.5 8.1 %collective-permute-start.15 = (bf16[128,768]{0,1:T(8,128)(2,1)S(1)}, bf16[128,768]{0,1:T(8,128)(2,1)S(1)}, u32[]{:S(2)}, u32[]{:S(2)}) collective-permute-start(bf16[128,768]{0,1:T(8,128)(2,1)S(1)} %convolution_convert_fusion.8), channel_id=1, source_target_pairs={{0,8},{4,12},{8,0},{12,4},{16,24},{20,28},{24,16},{28,20},{1,9},{5... | collective-permute-start | bytes 589832 | tf_op jit(solution)/shard_map/ppermute | solution.py:17
  61.8 7.1 %collective-permute-start.18 = (bf16[128,768]{0,1:T(8,128)(2,1)S(1)}, bf16[128,768]{0,1:T(8,128)(2,1)S(1)}, u32[]{:S(2)}, u32[]{:S(2)}) collective-permute-start(bf16[128,768]{0,1:T(8,128)(2,1)S(1)} %get-tuple-element.14), channel_id=1, source_target_pairs={{0,8},{4,12},{8,0},{12,4},{16,24},{20,28},{24,16},{28,20},{1,9},{5... | collective-permute-start | bytes 589832 | tf_op jit(solution)/shard_map/ppermute | solution.py:17
  63.0 8.8 %collective-permute-start.16 = (bf16[128,768]{0,1:T(8,128)(2,1)S(1)}, bf16[128,768]{0,1:T(8,128)(2,1)S(1)}, u32[]{:S(2)}, u32[]{:S(2)}) collective-permute-start(bf16[128,768]{0,1:T(8,128)(2,1)S(1)} %get-tuple-element.14), channel_id=1, source_target_pairs={{0,4},{4,0},{8,12},{12,8},{16,20},{20,16},{24,28},{28,24},{1,5},{5... | collective-permute-start | bytes 589832 | tf_op jit(solution)/shard_map/ppermute | solution.py:17
  63.1 6.3 %collective-permute-start.17 = (bf16[128,768]{0,1:T(8,128)(2,1)S(1)}, bf16[128,768]{0,1:T(8,128)(2,1)S(1)}, u32[]{:S(2)}, u32[]{:S(2)}) collective-permute-start(bf16[128,768]{0,1:T(8,128)(2,1)S(1)} %convolution_convert_fusion.7), channel_id=1, source_target_pairs={{0,4},{4,0},{8,12},{12,8},{16,20},{20,16},{24,28},{28,24},{1,5},{5... | collective-permute-start | bytes 589832 | tf_op jit(solution)/shard_map/ppermute | solution.py:17
  63.6 8.2 %collective-permute-start.19 = (bf16[128,768]{0,1:T(8,128)(2,1)S(1)}, bf16[128,768]{0,1:T(8,128)(2,1)S(1)}, u32[]{:S(2)}, u32[]{:S(2)}) collective-permute-start(bf16[128,768]{0,1:T(8,128)(2,1)S(1)} %convolution_convert_fusion.6), channel_id=1, source_target_pairs={{0,8},{4,12},{8,0},{12,4},{16,24},{20,28},{24,16},{28,20},{1,9},{5... | collective-permute-start | bytes 589832 | tf_op jit(solution)/shard_map/ppermute | solution.py:17
  72.8 7.0 %collective-permute-start.22 = (bf16[128,768]{0,1:T(8,128)(2,1)S(1)}, bf16[128,768]{0,1:T(8,128)(2,1)S(1)}, u32[]{:S(2)}, u32[]{:S(2)}) collective-permute-start(bf16[128,768]{0,1:T(8,128)(2,1)S(1)} %get-tuple-element.16), channel_id=1, source_target_pairs={{0,8},{4,12},{8,0},{12,4},{16,24},{20,28},{24,16},{28,20},{1,9},{5... | collective-permute-start | bytes 589832 | tf_op jit(solution)/shard_map/ppermute | solution.py:17
  74.1 8.7 %collective-permute-start.20 = (bf16[128,768]{0,1:T(8,128)(2,1)S(1)}, bf16[128,768]{0,1:T(8,128)(2,1)S(1)}, u32[]{:S(2)}, u32[]{:S(2)}) collective-permute-start(bf16[128,768]{0,1:T(8,128)(2,1)S(1)} %get-tuple-element.16), channel_id=1, source_target_pairs={{0,4},{4,0},{8,12},{12,8},{16,20},{20,16},{24,28},{28,24},{1,5},{5... | collective-permute-start | bytes 589832 | tf_op jit(solution)/shard_map/ppermute | solution.py:17
  74.2 6.2 %collective-permute-start.21 = (bf16[128,768]{0,1:T(8,128)(2,1)S(1)}, bf16[128,768]{0,1:T(8,128)(2,1)S(1)}, u32[]{:S(2)}, u32[]{:S(2)}) collective-permute-start(bf16[128,768]{0,1:T(8,128)(2,1)S(1)} %convolution_convert_fusion.5), channel_id=1, source_target_pairs={{0,4},{4,0},{8,12},{12,8},{16,20},{20,16},{24,28},{28,24},{1,5},{5... | collective-permute-start | bytes 589832 | tf_op jit(solution)/shard_map/ppermute | solution.py:17
  74.6 8.1 %collective-permute-start.23 = (bf16[128,768]{0,1:T(8,128)(2,1)S(1)}, bf16[128,768]{0,1:T(8,128)(2,1)S(1)}, u32[]{:S(2)}, u32[]{:S(2)}) collective-permute-start(bf16[128,768]{0,1:T(8,128)(2,1)S(1)} %convolution_convert_fusion.4), channel_id=1, source_target_pairs={{0,8},{4,12},{8,0},{12,4},{16,24},{20,28},{24,16},{28,20},{1,9},{5... | collective-permute-start | bytes 589832 | tf_op jit(solution)/shard_map/ppermute | solution.py:17
  83.9 6.1 %collective-permute-start.26 = (bf16[128,768]{0,1:T(8,128)(2,1)S(1)}, bf16[128,768]{0,1:T(8,128)(2,1)S(1)}, u32[]{:S(2)}, u32[]{:S(2)}) collective-permute-start(bf16[128,768]{0,1:T(8,128)(2,1)S(1)} %get-tuple-element.18), channel_id=1, source_target_pairs={{0,8},{4,12},{8,0},{12,4},{16,24},{20,28},{24,16},{28,20},{1,9},{5... | collective-permute-start | bytes 589832 | tf_op jit(solution)/shard_map/ppermute | solution.py:17
  85.9 7.9 %collective-permute-start.24 = (bf16[128,768]{0,1:T(8,128)(2,1)S(1)}, bf16[128,768]{0,1:T(8,128)(2,1)S(1)}, u32[]{:S(2)}, u32[]{:S(2)}) collective-permute-start(bf16[128,768]{0,1:T(8,128)(2,1)S(1)} %get-tuple-element.18), channel_id=1, source_target_pairs={{0,4},{4,0},{8,12},{12,8},{16,20},{20,16},{24,28},{28,24},{1,5},{5... | collective-permute-start | bytes 589832 | tf_op jit(solution)/shard_map/ppermute | solution.py:17
  86.0 4.5 %collective-permute-start.25 = (bf16[128,768]{0,1:T(8,128)(2,1)S(1)}, bf16[128,768]{0,1:T(8,128)(2,1)S(1)}, u32[]{:S(2)}, u32[]{:S(2)}) collective-permute-start(bf16[128,768]{0,1:T(8,128)(2,1)S(1)} %convolution_convert_fusion.3), channel_id=1, source_target_pairs={{0,4},{4,0},{8,12},{12,8},{16,20},{20,16},{24,28},{28,24},{1,5},{5... | collective-permute-start | bytes 589832 | tf_op jit(solution)/shard_map/ppermute | solution.py:17
  86.5 7.3 %collective-permute-start.27 = (bf16[128,768]{0,1:T(8,128)(2,1)S(1)}, bf16[128,768]{0,1:T(8,128)(2,1)S(1)}, u32[]{:S(2)}, u32[]{:S(2)}) collective-permute-start(bf16[128,768]{0,1:T(8,128)(2,1)S(1)} %convolution_convert_fusion.2), channel_id=1, source_target_pairs={{0,8},{4,12},{8,0},{12,4},{16,24},{20,28},{24,16},{28,20},{1,9},{5... | collective-permute-start | bytes 589832 | tf_op jit(solution)/shard_map/ppermute | solution.py:17
  95.5 7.9 %collective-permute-start.30 = (bf16[128,768]{0,1:T(8,128)(2,1)S(1)}, bf16[128,768]{0,1:T(8,128)(2,1)S(1)}, u32[]{:S(2)}, u32[]{:S(2)}) collective-permute-start(bf16[128,768]{0,1:T(8,128)(2,1)S(1)} %get-tuple-element.20), channel_id=1, source_target_pairs={{0,8},{4,12},{8,0},{12,4},{16,24},{20,28},{24,16},{28,20},{1,9},{5... | collective-permute-start | bytes 589832 | tf_op jit(solution)/shard_map/ppermute | solution.py:17
  97.1 9.2 %collective-permute-start.28 = (bf16[128,768]{0,1:T(8,128)(2,1)S(1)}, bf16[128,768]{0,1:T(8,128)(2,1)S(1)}, u32[]{:S(2)}, u32[]{:S(2)}) collective-permute-start(bf16[128,768]{0,1:T(8,128)(2,1)S(1)} %get-tuple-element.20), channel_id=1, source_target_pairs={{0,4},{4,0},{8,12},{12,8},{16,20},{20,16},{24,28},{28,24},{1,5},{5... | collective-permute-start | bytes 589832 | tf_op jit(solution)/shard_map/ppermute | solution.py:17
  97.1 6.8 %collective-permute-start.29 = (bf16[128,768]{0,1:T(8,128)(2,1)S(1)}, bf16[128,768]{0,1:T(8,128)(2,1)S(1)}, u32[]{:S(2)}, u32[]{:S(2)}) collective-permute-start(bf16[128,768]{0,1:T(8,128)(2,1)S(1)} %convolution_convert_fusion.1), channel_id=1, source_target_pairs={{0,4},{4,0},{8,12},{12,8},{16,20},{20,16},{24,28},{28,24},{1,5},{5... | collective-permute-start | bytes 589832 | tf_op jit(solution)/shard_map/ppermute | solution.py:17
  97.6 8.7 %collective-permute-start.31 = (bf16[128,768]{0,1:T(8,128)(2,1)S(1)}, bf16[128,768]{0,1:T(8,128)(2,1)S(1)}, u32[]{:S(2)}, u32[]{:S(2)}) collective-permute-start(bf16[128,768]{0,1:T(8,128)(2,1)S(1)} %convolution_convert_fusion), channel_id=1, source_target_pairs={{0,8},{4,12},{8,0},{12,4},{16,24},{20,28},{24,16},{28,20},{1,9},{5... | collective-permute-start | bytes 589832 | tf_op jit(solution)/shard_map/ppermute | solution.py:17
  106.3 19.4 %copy-start.5 = (bf16[4,512,128]{2,1,0:T(8,128)(2,1)S(1)}, bf16[4,512,128]{2,1,0:T(8,128)(2,1)}, u32[]{:S(2)}) copy-start(bf16[4,512,128]{2,1,0:T(8,128)(2,1)} %param.11) | copy-start | bytes 1572868
